TPU v7x, 256 devices: a whole 4x4x8 slice. The times are simulated.
256 devices in a mesh: span: 8 (over y, x_hi), tm: 32 (over x_lo, z, core).
Axes of the slice: x: 4 (x_hi: 2, x_lo: 2; x = x_hi * 2 + x_lo), y: 4, z: 8, core: 2. Of those that a mesh axis runs over, the one named last changes fastest.
Arguments:
- launched: float32 [8, 2, 110, 8192], P(None, None, None, 'tm'), may hold values from -1.5 to 1.5
- coupling: float32 [8, 2, 2, 2, 110, 110], P('span'), may hold values from -2 to 2
- impulse: float32 [8, 2, 2, 2, 129], P('span'), may hold values from -1.5 to 1.5
- amplifier: float32 [8, 2, 110], P('span'), may hold values from 0.9 to 1.11
- nonlinear: float32 [8, 2, 2], P('span'), may hold values from 0.002 to 0.008
Outputs:
- monitored: float32 [8, 8, 2, 110, 8192], P('span', None, None, None, 'tm')
All inputs are finite; a program needn't handle non-finite values.
Results may differ from a plain program's by a relative error of at most 0.0004.
Values sent between devices are 32-bit elements; how exact they have to be, the bound alone decides.
No kernel may reach another device: no remote copies, remote signals or barrier semaphores. Data moves between devices by JAX's collectives and lax.ppermute only.
A program may use at most 64 MiB of HBM per device.

v0:
```python
import jax
import jax.numpy as jnp
from jax import lax
from jax.sharding import PartitionSpec as P


def band(values, width):
    padded = jnp.concatenate([values, jnp.zeros((width,), jnp.float32)])
    tiled = jnp.tile(padded, width)[: width * 2 * width]
    return tiled.reshape(width, 2 * width).T


def prepare(coupling_group, impulse_group):
    half_taps = (impulse_group.shape[-1] - 1) // 2
    width = 2 * half_taps

    def toeplitz(pair):
        real_band = band(pair[0], width)
        imag_band = band(pair[1], width)
        upper = jnp.concatenate([real_band, imag_band], axis=1)
        lower = jnp.concatenate([-imag_band, real_band], axis=1)
        return jnp.concatenate([upper, lower], axis=0)

    filters = jax.vmap(jax.vmap(toeplitz))(impulse_group)
    real_part = coupling_group[:, :, 0]
    imag_part = coupling_group[:, :, 1]
    upper = jnp.concatenate([real_part, -imag_part], axis=-1)
    lower = jnp.concatenate([imag_part, real_part], axis=-1)
    return (filters, jnp.concatenate([upper, lower], axis=-2))


def disperse(extended, matrix, half_taps):
    width = 2 * half_taps
    frames, _, channels, extent = extended.shape
    block_count = extent // width - 1
    blocks = extended.reshape(frames, 2, channels, block_count + 1, width)
    windows = jnp.concatenate([blocks[..., :-1, :], blocks[..., 1:, :]], axis=-1)
    stacked = jnp.concatenate([windows[:, 0], windows[:, 1]], axis=-1)
    product = jnp.einsum("fcbu,uv->fcbv", stacked, matrix, precision=lax.Precision.HIGHEST)
    real_part = product[..., :width].reshape(frames, channels, block_count * width)
    imag_part = product[..., width:].reshape(frames, channels, block_count * width)
    return jnp.stack([real_part, imag_part], axis=1)


def couple(signal, mixer, coefficient):
    frames, _, channels, extent = signal.shape
    flat = signal.reshape(frames, 2 * channels, extent)
    mixed = jnp.einsum("de,fel->fdl", mixer, flat, precision=lax.Precision.HIGHEST).reshape(
        frames, 2, channels, extent
    )
    power = jnp.sum(mixed * mixed, axis=(1, 2))
    phase = coefficient * power[:, None, :]
    cosine = jnp.cos(phase)
    sine = jnp.sin(phase)
    real_part = mixed[:, 0]
    imag_part = mixed[:, 1]
    return jnp.stack(
        [real_part * cosine - imag_part * sine, real_part * sine + imag_part * cosine], axis=1
    )


def neighbours(block, halo):
    count = lax.axis_size("tm")
    forward = [(i, i + 1) for i in range(count - 1)]
    backward = [(i + 1, i) for i in range(count - 1)]
    extent = block.shape[-1]
    low = lax.ppermute(lax.slice_in_dim(block, extent - halo, None, axis=3), "tm", forward)
    high = lax.ppermute(lax.slice_in_dim(block, 0, halo, axis=3), "tm", backward)
    return jnp.concatenate([low, block, high], axis=3)


def group_pass(signal, filters, mixers, amplifier_group, nonlinear_group, origin, length):
    span_count, step_count = nonlinear_group.shape
    half_taps = filters.shape[-1] // 4
    halo = span_count * step_count * half_taps
    extent = signal.shape[-1]
    signal = neighbours(signal, halo)
    offset = -halo
    for span_index in range(span_count):
        for step_index in range(step_count):
            signal = disperse(signal, filters[span_index, step_index], half_taps)
            offset = offset + half_taps
            where = origin + offset + jnp.arange(signal.shape[-1], dtype=jnp.int32)
            inside = ((where >= 0) & (where < length)).astype(jnp.float32)
            signal = signal * inside
            signal = couple(
                signal, mixers[span_index, step_index], nonlinear_group[span_index, step_index]
            )
        signal = signal * amplifier_group[span_index][None, None, :, None]
    assert signal.shape[-1] == extent
    return signal


def shards(launched, coupling, impulse, amplifier, nonlinear):
    sections = lax.axis_size("span")
    section_index = lax.axis_index("span")
    frames_count, _, _, extent = launched.shape
    per_section = frames_count // sections
    length = extent * lax.axis_size("tm")
    origin = lax.axis_index("tm") * extent
    coupling_all = lax.all_gather(coupling, "span", axis=0, tiled=True)
    impulse_all = lax.all_gather(impulse, "span", axis=0, tiled=True)
    amplifier_all = lax.all_gather(amplifier, "span", axis=0, tiled=True)
    nonlinear_all = lax.all_gather(nonlinear, "span", axis=0, tiled=True)
    signal = lax.dynamic_slice_in_dim(launched, section_index * per_section, per_section, 0)

    def advance(signal, params):
        coupling_group, impulse_group, amplifier_group, nonlinear_group = params
        filters, mixers = prepare(coupling_group, impulse_group)
        signal = group_pass(
            signal, filters, mixers, amplifier_group, nonlinear_group, origin, length
        )
        return (signal, signal)

    _, stacked = lax.scan(
        advance, signal, (coupling_all, impulse_all, amplifier_all, nonlinear_all)
    )
    return lax.all_to_all(stacked, "span", 0, 1, tiled=True)


def solution(mesh):
    placed = (
        P(None, None, None, "tm"),
        P("span", None, None, None, None, None),
        P("span", None, None, None, None),
        P("span", None, None),
        P("span", None, None),
    )
    return jax.shard_map(
        shards,
        mesh=mesh,
        in_specs=placed,
        out_specs=P("span", None, None, None, "tm"),
        check_vma=False,
    )
```

profile of v0, /device:TPU:2, one launch (start us, length us, event | category | flops | bytes accessed | tf_op | source)
XLA Modules:
  0.0 689.6 jit_solution(1994653478486105164)
XLA Ops:
  8.7 22.9 %all_gather.14 = f32[8,2,2]{2,1,0:T(2,128)S(1)} all-gather(f32[1,2,2]{2,1,0:T(2,128)} %param.11), channel_id=1, replica_groups=mesh['span'=8,'tm'=32] {'span'}, dimensions={0}, use_global_device_ids=true | all-gather | bytes 144 | tf_op jit(solution)/shard_map/all_gather | solution.py:104
  31.7 18.4 %all_gather.15 = f32[8,2,110]{2,1,0:T(2,128)S(1)} all-gather(f32[1,2,110]{2,1,0:T(2,128)} %param.10), channel_id=1, replica_groups=mesh['span'=8,'tm'=32] {'span'}, dimensions={0}, use_global_device_ids=true | all-gather | bytes 7920 | tf_op jit(solution)/shard_map/all_gather | solution.py:103
  50.1 37.0 %all_gather.12 = f32[8,2,2,2,129]{4,3,2,1,0:T(2,128)} all-gather(f32[1,2,2,2,129]{4,3,2,1,0:T(2,128)} %param.9), channel_id=1, replica_groups=mesh['span'=8,'tm'=32] {'span'}, dimensions={0}, use_global_device_ids=true | all-gather | bytes 37152 | tf_op jit(solution)/shard_map/all_gather | solution.py:102
  87.1 568.2 %while.13 = (s32[]{:T(128)}, f32[1,2,110,256]{3,2,1,0:T(8,128)}, f32[8,1,2,110,256]{4,2,3,1,0:T(2,128)}, f32[8,2,2,2,129]{4,3,2,1,0:T(2,128)}, s32[]{:T(128)}, /...) while((s32[]{:T(128)}, f32[1,2,110,256]{3,2,1,0:T(8,128)}, ...), condition=%wide.region_5.6_spmd, body=%wide.region_0.5_spmd.sunk | while | flops 3470978304 | bytes 83243504 | solution.py:115
  89.0 2.4 collective-permute-start.1
  106.0 2.7 maximum_maximum_fusion.4
  138.9 2.4 multiply_reduce_fusion.9
  154.8 8.4 %collective-permute-start = (f32[1,2,110,256]{3,2,1,0:T(8,128)}, f32[1,2,110,256]{3,2,1,0:T(8,128)}, u32[]{:S(2)}, u32[]{:S(2)}) collective-permute-start(f32[1,2,110,256]{3,2,1,0:T(8,128)} %get-tuple-element.367), channel_id=1, source_target_pairs={{1,0},{2,1},{3,2},{4,3},{5,4},{6,5},{7,6},{8,7},{9,8},{10,9},{11,1... | collective-permute-start | bytes 675848 | tf_op jit(solution)/shard_map/while/body/eval_jaxpr/ppermute | solution.py:68
  179.8 2.7 maximum_maximum_fusion.4
  212.6 2.4 multiply_reduce_fusion.9
  228.6 5.7 collective-permute-start
  245.8 2.3 reshape.881
  250.9 2.7 maximum_maximum_fusion.4
  283.7 2.4 multiply_reduce_fusion.9
  299.7 5.7 collective-permute-start
  322.0 2.7 maximum_maximum_fusion.4
  354.8 2.4 multiply_reduce_fusion.9
  370.8 5.7 collective-permute-start
  388.0 2.3 reshape.881
  393.1 2.7 maximum_maximum_fusion.4
  426.0 2.4 multiply_reduce_fusion.9
  441.9 5.7 collective-permute-start
  459.1 2.3 reshape.881
  464.2 2.7 maximum_maximum_fusion.4
  497.1 2.4 multiply_reduce_fusion.9
  513.0 5.7 collective-permute-start
  535.3 2.7 maximum_maximum_fusion.4
  568.2 2.4 multiply_reduce_fusion.9
  584.1 5.7 collective-permute-start
  606.4 2.7 maximum_maximum_fusion.4
  639.3 2.4 multiply_reduce_fusion.9
  655.2 26.3 %all_to_all.12 = f32[8,1,2,110,256]{4,2,3,1,0:T(2,128)S(1)} all-to-all(f32[8,1,2,110,256]{4,2,3,1,0:T(2,128)} %get-tuple-element.90), channel_id=1, replica_groups=mesh['span'=8,'tm'=32] {'span'}, dimensions={0} | all-to-all | bytes 3604480 | tf_op jit(solution)/shard_map/all_to_all | solution.py:118
  (894 shorter events, 475.0 us)
Async XLA Ops:
  6.5 80.5 %all-gather.2.cloned.1.call-start = ((), (), s32[]{:S(2)}) async-start(), calls=%async_computation.1 | async-start | bytes 4055040 | tf_op jit(solution)/shard_map/all_gather | solution.py:101
  87.1 22.0 %collective-permute-start = (f32[1,2,110,256]{3,2,1,0:T(8,128)}, f32[1,2,110,256]{3,2,1,0:T(8,128)}, u32[]{:S(2)}, u32[]{:S(2)}) collective-permute-start(f32[1,2,110,256]{3,2,1,0:T(8,128)} %get-tuple-element.367), channel_id=1, source_target_pairs={{1,0},{2,1},{3,2},{4,3},{5,4},{6,5},{7,6},{8,7},{9,8},{10,9},{11,1... | collective-permute-start | bytes 675848 | tf_op jit(solution)/shard_map/while/body/eval_jaxpr/ppermute | solution.py:68
  89.0 20.1 %collective-permute-start.1 = (f32[1,2,110,256]{3,2,1,0:T(8,128)}, f32[1,2,110,256]{3,2,1,0:T(8,128)}, u32[]{:S(2)}, u32[]{:S(2)}) collective-permute-start(f32[1,2,110,256]{3,2,1,0:T(8,128)} %get-tuple-element.367), channel_id=1, source_target_pairs={{0,1},{1,2},{2,3},{3,4},{4,5},{5,6},{6,7},{7,8},{8,9},{9,10},{10,1... | collective-permute-start | bytes 675848 | tf_op jit(solution)/shard_map/while/body/eval_jaxpr/ppermute | solution.py:67
  99.1 7.0 %copy-start.1 = (f32[2,2,256,128]{3,2,1,0:T(8,128)S(1)}, f32[2,2,256,128]{3,2,1,0:T(8,128)}, u32[]{:S(2)}) copy-start(f32[2,2,256,128]{3,2,1,0:T(8,128)} %bitcast_negate_fusion.2) | copy-start | bytes 1572868 | tf_op jit(solution)/shard_map/while
  105.4 3.3 copy-start.4
  154.8 27.9 %collective-permute-start = (f32[1,2,110,256]{3,2,1,0:T(8,128)}, f32[1,2,110,256]{3,2,1,0:T(8,128)}, u32[]{:S(2)}, u32[]{:S(2)}) collective-permute-start(f32[1,2,110,256]{3,2,1,0:T(8,128)} %get-tuple-element.367), channel_id=1, source_target_pairs={{1,0},{2,1},{3,2},{4,3},{5,4},{6,5},{7,6},{8,7},{9,8},{10,9},{11,1... | collective-permute-start | bytes 675848 | tf_op jit(solution)/shard_map/while/body/eval_jaxpr/ppermute | solution.py:68
  163.2 19.6 %collective-permute-start.1 = (f32[1,2,110,256]{3,2,1,0:T(8,128)}, f32[1,2,110,256]{3,2,1,0:T(8,128)}, u32[]{:S(2)}, u32[]{:S(2)}) collective-permute-start(f32[1,2,110,256]{3,2,1,0:T(8,128)} %get-tuple-element.367), channel_id=1, source_target_pairs={{0,1},{1,2},{2,3},{3,4},{4,5},{5,6},{6,7},{7,8},{8,9},{9,10},{10,1... | collective-permute-start | bytes 675848 | tf_op jit(solution)/shard_map/while/body/eval_jaxpr/ppermute | solution.py:67
  172.8 7.0 %copy-start.1 = (f32[2,2,256,128]{3,2,1,0:T(8,128)S(1)}, f32[2,2,256,128]{3,2,1,0:T(8,128)}, u32[]{:S(2)}) copy-start(f32[2,2,256,128]{3,2,1,0:T(8,128)} %bitcast_negate_fusion.2) | copy-start | bytes 1572868 | tf_op jit(solution)/shard_map/while
  179.1 3.3 copy-start.4
  228.6 25.3 %collective-permute-start = (f32[1,2,110,256]{3,2,1,0:T(8,128)}, f32[1,2,110,256]{3,2,1,0:T(8,128)}, u32[]{:S(2)}, u32[]{:S(2)}) collective-permute-start(f32[1,2,110,256]{3,2,1,0:T(8,128)} %get-tuple-element.367), channel_id=1, source_target_pairs={{1,0},{2,1},{3,2},{4,3},{5,4},{6,5},{7,6},{8,7},{9,8},{10,9},{11,1... | collective-permute-start | bytes 675848 | tf_op jit(solution)/shard_map/while/body/eval_jaxpr/ppermute | solution.py:68
  234.3 19.6 %collective-permute-start.1 = (f32[1,2,110,256]{3,2,1,0:T(8,128)}, f32[1,2,110,256]{3,2,1,0:T(8,128)}, u32[]{:S(2)}, u32[]{:S(2)}) collective-permute-start(f32[1,2,110,256]{3,2,1,0:T(8,128)} %get-tuple-element.367), channel_id=1, source_target_pairs={{0,1},{1,2},{2,3},{3,4},{4,5},{5,6},{6,7},{7,8},{8,9},{9,10},{10,1... | collective-permute-start | bytes 675848 | tf_op jit(solution)/shard_map/while/body/eval_jaxpr/ppermute | solution.py:67
  243.9 7.0 %copy-start.1 = (f32[2,2,256,128]{3,2,1,0:T(8,128)S(1)}, f32[2,2,256,128]{3,2,1,0:T(8,128)}, u32[]{:S(2)}) copy-start(f32[2,2,256,128]{3,2,1,0:T(8,128)} %bitcast_negate_fusion.2) | copy-start | bytes 1572868 | tf_op jit(solution)/shard_map/while
  250.2 3.3 copy-start.4
  299.7 25.3 %collective-permute-start = (f32[1,2,110,256]{3,2,1,0:T(8,128)}, f32[1,2,110,256]{3,2,1,0:T(8,128)}, u32[]{:S(2)}, u32[]{:S(2)}) collective-permute-start(f32[1,2,110,256]{3,2,1,0:T(8,128)} %get-tuple-element.367), channel_id=1, source_target_pairs={{1,0},{2,1},{3,2},{4,3},{5,4},{6,5},{7,6},{8,7},{9,8},{10,9},{11,1... | collective-permute-start | bytes 675848 | tf_op jit(solution)/shard_map/while/body/eval_jaxpr/ppermute | solution.py:68
  305.4 19.6 %collective-permute-start.1 = (f32[1,2,110,256]{3,2,1,0:T(8,128)}, f32[1,2,110,256]{3,2,1,0:T(8,128)}, u32[]{:S(2)}, u32[]{:S(2)}) collective-permute-start(f32[1,2,110,256]{3,2,1,0:T(8,128)} %get-tuple-element.367), channel_id=1, source_target_pairs={{0,1},{1,2},{2,3},{3,4},{4,5},{5,6},{6,7},{7,8},{8,9},{9,10},{10,1... | collective-permute-start | bytes 675848 | tf_op jit(solution)/shard_map/while/body/eval_jaxpr/ppermute | solution.py:67
  315.0 7.0 %copy-start.1 = (f32[2,2,256,128]{3,2,1,0:T(8,128)S(1)}, f32[2,2,256,128]{3,2,1,0:T(8,128)}, u32[]{:S(2)}) copy-start(f32[2,2,256,128]{3,2,1,0:T(8,128)} %bitcast_negate_fusion.2) | copy-start | bytes 1572868 | tf_op jit(solution)/shard_map/while
  321.3 3.3 copy-start.4
  370.8 25.3 %collective-permute-start = (f32[1,2,110,256]{3,2,1,0:T(8,128)}, f32[1,2,110,256]{3,2,1,0:T(8,128)}, u32[]{:S(2)}, u32[]{:S(2)}) collective-permute-start(f32[1,2,110,256]{3,2,1,0:T(8,128)} %get-tuple-element.367), channel_id=1, source_target_pairs={{1,0},{2,1},{3,2},{4,3},{5,4},{6,5},{7,6},{8,7},{9,8},{10,9},{11,1... | collective-permute-start | bytes 675848 | tf_op jit(solution)/shard_map/while/body/eval_jaxpr/ppermute | solution.py:68
  376.5 19.6 %collective-permute-start.1 = (f32[1,2,110,256]{3,2,1,0:T(8,128)}, f32[1,2,110,256]{3,2,1,0:T(8,128)}, u32[]{:S(2)}, u32[]{:S(2)}) collective-permute-start(f32[1,2,110,256]{3,2,1,0:T(8,128)} %get-tuple-element.367), channel_id=1, source_target_pairs={{0,1},{1,2},{2,3},{3,4},{4,5},{5,6},{6,7},{7,8},{8,9},{9,10},{10,1... | collective-permute-start | bytes 675848 | tf_op jit(solution)/shard_map/while/body/eval_jaxpr/ppermute | solution.py:67
  386.1 7.0 %copy-start.1 = (f32[2,2,256,128]{3,2,1,0:T(8,128)S(1)}, f32[2,2,256,128]{3,2,1,0:T(8,128)}, u32[]{:S(2)}) copy-start(f32[2,2,256,128]{3,2,1,0:T(8,128)} %bitcast_negate_fusion.2) | copy-start | bytes 1572868 | tf_op jit(solution)/shard_map/while
  441.9 25.3 %collective-permute-start = (f32[1,2,110,256]{3,2,1,0:T(8,128)}, f32[1,2,110,256]{3,2,1,0:T(8,128)}, u32[]{:S(2)}, u32[]{:S(2)}) collective-permute-start(f32[1,2,110,256]{3,2,1,0:T(8,128)} %get-tuple-element.367), channel_id=1, source_target_pairs={{1,0},{2,1},{3,2},{4,3},{5,4},{6,5},{7,6},{8,7},{9,8},{10,9},{11,1... | collective-permute-start | bytes 675848 | tf_op jit(solution)/shard_map/while/body/eval_jaxpr/ppermute | solution.py:68
  447.6 19.6 %collective-permute-start.1 = (f32[1,2,110,256]{3,2,1,0:T(8,128)}, f32[1,2,110,256]{3,2,1,0:T(8,128)}, u32[]{:S(2)}, u32[]{:S(2)}) collective-permute-start(f32[1,2,110,256]{3,2,1,0:T(8,128)} %get-tuple-element.367), channel_id=1, source_target_pairs={{0,1},{1,2},{2,3},{3,4},{4,5},{5,6},{6,7},{7,8},{8,9},{9,10},{10,1... | collective-permute-start | bytes 675848 | tf_op jit(solution)/shard_map/while/body/eval_jaxpr/ppermute | solution.py:67
  457.2 7.0 %copy-start.1 = (f32[2,2,256,128]{3,2,1,0:T(8,128)S(1)}, f32[2,2,256,128]{3,2,1,0:T(8,128)}, u32[]{:S(2)}) copy-start(f32[2,2,256,128]{3,2,1,0:T(8,128)} %bitcast_negate_fusion.2) | copy-start | bytes 1572868 | tf_op jit(solution)/shard_map/while
  463.5 3.3 copy-start.4
  513.0 25.3 %collective-permute-start = (f32[1,2,110,256]{3,2,1,0:T(8,128)}, f32[1,2,110,256]{3,2,1,0:T(8,128)}, u32[]{:S(2)}, u32[]{:S(2)}) collective-permute-start(f32[1,2,110,256]{3,2,1,0:T(8,128)} %get-tuple-element.367), channel_id=1, source_target_pairs={{1,0},{2,1},{3,2},{4,3},{5,4},{6,5},{7,6},{8,7},{9,8},{10,9},{11,1... | collective-permute-start | bytes 675848 | tf_op jit(solution)/shard_map/while/body/eval_jaxpr/ppermute | solution.py:68
  518.8 19.6 %collective-permute-start.1 = (f32[1,2,110,256]{3,2,1,0:T(8,128)}, f32[1,2,110,256]{3,2,1,0:T(8,128)}, u32[]{:S(2)}, u32[]{:S(2)}) collective-permute-start(f32[1,2,110,256]{3,2,1,0:T(8,128)} %get-tuple-element.367), channel_id=1, source_target_pairs={{0,1},{1,2},{2,3},{3,4},{4,5},{5,6},{6,7},{7,8},{8,9},{9,10},{10,1... | collective-permute-start | bytes 675848 | tf_op jit(solution)/shard_map/while/body/eval_jaxpr/ppermute | solution.py:67
  528.3 7.0 %copy-start.1 = (f32[2,2,256,128]{3,2,1,0:T(8,128)S(1)}, f32[2,2,256,128]{3,2,1,0:T(8,128)}, u32[]{:S(2)}) copy-start(f32[2,2,256,128]{3,2,1,0:T(8,128)} %bitcast_negate_fusion.2) | copy-start | bytes 1572868 | tf_op jit(solution)/shard_map/while
  534.6 3.3 copy-start.4
  584.1 25.3 %collective-permute-start = (f32[1,2,110,256]{3,2,1,0:T(8,128)}, f32[1,2,110,256]{3,2,1,0:T(8,128)}, u32[]{:S(2)}, u32[]{:S(2)}) collective-permute-start(f32[1,2,110,256]{3,2,1,0:T(8,128)} %get-tuple-element.367), channel_id=1, source_target_pairs={{1,0},{2,1},{3,2},{4,3},{5,4},{6,5},{7,6},{8,7},{9,8},{10,9},{11,1... | collective-permute-start | bytes 675848 | tf_op jit(solution)/shard_map/while/body/eval_jaxpr/ppermute | solution.py:68
  589.9 19.6 %collective-permute-start.1 = (f32[1,2,110,256]{3,2,1,0:T(8,128)}, f32[1,2,110,256]{3,2,1,0:T(8,128)}, u32[]{:S(2)}, u32[]{:S(2)}) collective-permute-start(f32[1,2,110,256]{3,2,1,0:T(8,128)} %get-tuple-element.367), channel_id=1, source_target_pairs={{0,1},{1,2},{2,3},{3,4},{4,5},{5,6},{6,7},{7,8},{8,9},{9,10},{10,1... | collective-permute-start | bytes 675848 | tf_op jit(solution)/shard_map/while/body/eval_jaxpr/ppermute | solution.py:67
  599.4 7.0 %copy-start.1 = (f32[2,2,256,128]{3,2,1,0:T(8,128)S(1)}, f32[2,2,256,128]{3,2,1,0:T(8,128)}, u32[]{:S(2)}) copy-start(f32[2,2,256,128]{3,2,1,0:T(8,128)} %bitcast_negate_fusion.2) | copy-start | bytes 1572868 | tf_op jit(solution)/shard_map/while
  605.7 3.3 copy-start.4
  (18 other events, 58.2 us)
Sparse Core Ops, SparseCore 0:
  9.9 74.1 all-gather.1
where the time goes:
time: 698 us; the launch traced here: 690 us
  local copies, waits for them, and re-layouts  275 us (39%)
  other arithmetic  132 us (19%)
  blocking collectives  105 us (15%)
  matrix products  98.7 us (14%)
  starting transfers between devices  60.5 us (9%)
  between operations  13.4 us (2%)
    dot_general x32, matrix products, disperse(): jnp.einsum('fcbu,uv->fcbv', stacked, matrix, precision=lax.Precision.HIGH...  59.1 us
    ppermute x8, starting transfers between devices, neighbours(): lax.ppermute(lax.slice_in_dim(block, 0, halo, axis=3), 'tm', backward)  44.6 us
    reshape x32, local copies, waits for them, and re-layouts, band(): return tiled.reshape(width, 2 * width).T  40 us
    dot_general x32, matrix products, couple(): jnp.einsum('de,fel->fdl', mixer, flat, precision=lax.Precision.HIGHEST)  39.6 us
    all_gather x1, blocking collectives, shards(): impulse_all = lax.all_gather(impulse, 'span', axis=0, tiled=True)  37 us
    while x80, local copies, waits for them, and re-layouts  28.2 us
    all_to_all x1, blocking collectives, shards(): return lax.all_to_all(stacked, 'span', 0, 1, tiled=True)  26.3 us
    mul x32, other arithmetic, group_pass(): signal = signal * inside  26.3 us
  transfers between devices with their start and end apart: 17, of which 0 were waited for; matrix products, arithmetic and copies ran while one was open for 20% of the time, Pallas kernels for 0%

commit v1 on v0

--- a/solution.py
+++ b/solution.py
@@ -115,7 +115,10 @@
     _, stacked = lax.scan(
         advance, signal, (coupling_all, impulse_all, amplifier_all, nonlinear_all)
     )
-    return lax.all_to_all(stacked, "span", 0, 1, tiled=True)
+    return jnp.concatenate(
+        lax.all_to_all(jnp.stack(jnp.split(stacked, lax.axis_size("span"), axis=0)), "span", 0, 0),
+        axis=1,
+    )
 
 
 def solution(mesh):

time: 698 us -> 673 us (0.964)
  local copies, waits for them, and re-layouts: 275 us -> 259 us
  other arithmetic: 132 us -> 125 us
    reshape x32, local copies, waits for them, and re-layouts: 40 us -> 25.1 us  [band(): return tiled.reshape(width, 2 * width).T]
    concatenate x8, other arithmetic: 21.3 us -> 11.9 us  [toeplitz(): return jnp.concatenate([upper, lower], axis=0)]
  transfers between devices with their start and end apart: 17 -> 17, of which waited for: 0 -> 0; matrix products, arithmetic and copies ran while one was open for 20% -> 17% of each run, Pallas kernels for 0% -> 0%
where the time goes in v1:
time: 673 us; the launch traced here: 665 us
  local copies, waits for them, and re-layouts  259 us (38%)
  other arithmetic  125 us (19%)
  blocking collectives  104 us (15%)
  matrix products  98.5 us (15%)
  starting transfers between devices  60.6 us (9%)
  between operations  13.5 us (2%)
    dot_general x32, matrix products, disperse(): jnp.einsum('fcbu,uv->fcbv', stacked, matrix, precision=lax.Precision.HIGH...  59 us
    ppermute x8, starting transfers between devices, neighbours(): lax.ppermute(lax.slice_in_dim(block, 0, halo, axis=3), 'tm', backward)  44.8 us
    dot_general x32, matrix products, couple(): jnp.einsum('de,fel->fdl', mixer, flat, precision=lax.Precision.HIGHEST)  39.6 us
    all_gather x1, blocking collectives, shards(): impulse_all = lax.all_gather(impulse, 'span', axis=0, tiled=True)  37 us
    while x80, local copies, waits for them, and re-layouts  28.3 us
    mul x32, other arithmetic, group_pass(): signal = signal * inside  26.3 us
    all_to_all x1, blocking collectives, shards(): lax.all_to_all(jnp.stack(jnp.split(stacked, lax.axis_size('span'), axis=0...  26.1 us
    mul x48, local copies, waits for them, and re-layouts, group_pass(): signal = signal * inside  26.1 us
  transfers between devices with their start and end apart: 17, of which 0 were waited for; matrix products, arithmetic and copies ran while one was open for 17% of the time, Pallas kernels for 0%

profile of v1, /device:TPU:2, one launch (start us, length us, event | category | flops | bytes accessed | tf_op | source)
XLA Modules:
  0.0 665.1 jit_solution(11647246389389233629)
XLA Ops:
  8.8 22.9 %all_gather.14 = f32[8,2,2]{2,1,0:T(2,128)S(1)} all-gather(f32[1,2,2]{2,1,0:T(2,128)} %param.11), channel_id=1, replica_groups=mesh['span'=8,'tm'=32] {'span'}, dimensions={0}, use_global_device_ids=true | all-gather | bytes 144 | tf_op jit(solution)/shard_map/all_gather | solution.py:104
  31.7 18.4 %all_gather.15 = f32[8,2,110]{2,1,0:T(2,128)S(1)} all-gather(f32[1,2,110]{2,1,0:T(2,128)} %param.10), channel_id=1, replica_groups=mesh['span'=8,'tm'=32] {'span'}, dimensions={0}, use_global_device_ids=true | all-gather | bytes 7920 | tf_op jit(solution)/shard_map/all_gather | solution.py:103
  50.2 37.0 %all_gather.12 = f32[8,2,2,2,129]{4,3,2,1,0:T(2,128)} all-gather(f32[1,2,2,2,129]{4,3,2,1,0:T(2,128)} %param.9), channel_id=1, replica_groups=mesh['span'=8,'tm'=32] {'span'}, dimensions={0}, use_global_device_ids=true | all-gather | bytes 37152 | tf_op jit(solution)/shard_map/all_gather | solution.py:102
  87.1 539.6 %while.13 = (s32[]{:T(128)}, f32[1,2,110,256]{3,2,1,0:T(8,128)}, f32[8,1,2,110,256]{4,2,3,1,0:T(2,128)}, f32[8,2,2,2,129]{4,3,2,1,0:T(2,128)}, s32[]{:T(128)}, /...) while((s32[]{:T(128)}, f32[1,2,110,256]{3,2,1,0:T(8,128)}, ...), condition=%wide.region_5.6_spmd, body=%wide.region_0.5_spmd.sunk | while | flops 3470978304 | bytes 83243504 | solution.py:115
  89.0 2.4 collective-permute-start.1
  111.4 2.2 copy.141
  114.7 2.1 convolution_bitcast_fusion.12
  135.2 2.4 multiply_reduce_fusion.9
  151.3 8.4 %collective-permute-start = (f32[1,2,110,256]{3,2,1,0:T(8,128)}, f32[1,2,110,256]{3,2,1,0:T(8,128)}, u32[]{:S(2)}, u32[]{:S(2)}) collective-permute-start(f32[1,2,110,256]{3,2,1,0:T(8,128)} %get-tuple-element.367), channel_id=1, source_target_pairs={{1,0},{2,1},{3,2},{4,3},{5,4},{6,5},{7,6},{8,7},{9,8},{10,9},{11,1... | collective-permute-start | bytes 675848 | tf_op jit(solution)/shard_map/while/body/eval_jaxpr/ppermute | solution.py:68
  181.5 2.2 copy.141
  184.8 2.1 convolution_bitcast_fusion.12
  205.4 2.4 multiply_reduce_fusion.9
  221.5 5.7 collective-permute-start
  249.1 2.2 copy.141
  272.9 2.4 multiply_reduce_fusion.9
  289.0 5.7 collective-permute-start
  316.6 2.2 copy.141
  340.5 2.4 multiply_reduce_fusion.9
  356.6 5.7 collective-permute-start
  384.2 2.2 copy.141
  387.5 2.1 convolution_bitcast_fusion.12
  408.0 2.4 multiply_reduce_fusion.9
  424.1 5.7 collective-permute-start
  451.7 2.2 copy.141
  475.6 2.4 multiply_reduce_fusion.9
  491.7 5.7 collective-permute-start
  519.2 2.2 copy.141
  543.1 2.4 multiply_reduce_fusion.9
  559.2 5.7 collective-permute-start
  586.8 2.2 copy.141
  610.7 2.4 multiply_reduce_fusion.9
  630.9 26.1 %all_to_all.5 = f32[8,1,1,2,110,256]{5,3,4,2,1,0:T(2,128)S(1)} all-to-all(f32[8,1,1,2,110,256]{5,3,4,2,1,0:T(2,128)S(1)} %bitcast_dynamic-update-slice_fusion), channel_id=1, replica_groups=mesh['span'=8,'tm'=32] {'span'}, dimensions={0} | all-to-all | bytes 3604480 | tf_op jit(solution)/shard_map/all_to_all | solution.py:119
  (904 shorter events, 454.8 us)
Async XLA Ops:
  6.5 80.6 %all-gather.2.cloned.1.call-start = ((), (), s32[]{:S(2)}) async-start(), calls=%async_computation.1 | async-start | bytes 4055040 | tf_op jit(solution)/shard_map/all_gather | solution.py:101
  87.1 18.2 %collective-permute-start = (f32[1,2,110,256]{3,2,1,0:T(8,128)}, f32[1,2,110,256]{3,2,1,0:T(8,128)}, u32[]{:S(2)}, u32[]{:S(2)}) collective-permute-start(f32[1,2,110,256]{3,2,1,0:T(8,128)} %get-tuple-element.367), channel_id=1, source_target_pairs={{1,0},{2,1},{3,2},{4,3},{5,4},{6,5},{7,6},{8,7},{9,8},{10,9},{11,1... | collective-permute-start | bytes 675848 | tf_op jit(solution)/shard_map/while/body/eval_jaxpr/ppermute | solution.py:68
  89.0 16.3 %collective-permute-start.1 = (f32[1,2,110,256]{3,2,1,0:T(8,128)}, f32[1,2,110,256]{3,2,1,0:T(8,128)}, u32[]{:S(2)}, u32[]{:S(2)}) collective-permute-start(f32[1,2,110,256]{3,2,1,0:T(8,128)} %get-tuple-element.367), channel_id=1, source_target_pairs={{0,1},{1,2},{2,3},{3,4},{4,5},{5,6},{6,7},{7,8},{8,9},{9,10},{10,1... | collective-permute-start | bytes 675848 | tf_op jit(solution)/shard_map/while/body/eval_jaxpr/ppermute | solution.py:67
  99.1 4.4 copy-start.1
  103.4 1.5 copy-start.2
  151.3 24.2 %collective-permute-start = (f32[1,2,110,256]{3,2,1,0:T(8,128)}, f32[1,2,110,256]{3,2,1,0:T(8,128)}, u32[]{:S(2)}, u32[]{:S(2)}) collective-permute-start(f32[1,2,110,256]{3,2,1,0:T(8,128)} %get-tuple-element.367), channel_id=1, source_target_pairs={{1,0},{2,1},{3,2},{4,3},{5,4},{6,5},{7,6},{8,7},{9,8},{10,9},{11,1... | collective-permute-start | bytes 675848 | tf_op jit(solution)/shard_map/while/body/eval_jaxpr/ppermute | solution.py:68
  159.7 15.8 %collective-permute-start.1 = (f32[1,2,110,256]{3,2,1,0:T(8,128)}, f32[1,2,110,256]{3,2,1,0:T(8,128)}, u32[]{:S(2)}, u32[]{:S(2)}) collective-permute-start(f32[1,2,110,256]{3,2,1,0:T(8,128)} %get-tuple-element.367), channel_id=1, source_target_pairs={{0,1},{1,2},{2,3},{3,4},{4,5},{5,6},{6,7},{7,8},{8,9},{9,10},{10,1... | collective-permute-start | bytes 675848 | tf_op jit(solution)/shard_map/while/body/eval_jaxpr/ppermute | solution.py:67
  169.2 4.4 copy-start.1
  173.6 1.5 copy-start.2
  221.5 21.5 %collective-permute-start = (f32[1,2,110,256]{3,2,1,0:T(8,128)}, f32[1,2,110,256]{3,2,1,0:T(8,128)}, u32[]{:S(2)}, u32[]{:S(2)}) collective-permute-start(f32[1,2,110,256]{3,2,1,0:T(8,128)} %get-tuple-element.367), channel_id=1, source_target_pairs={{1,0},{2,1},{3,2},{4,3},{5,4},{6,5},{7,6},{8,7},{9,8},{10,9},{11,1... | collective-permute-start | bytes 675848 | tf_op jit(solution)/shard_map/while/body/eval_jaxpr/ppermute | solution.py:68
  227.2 15.8 %collective-permute-start.1 = (f32[1,2,110,256]{3,2,1,0:T(8,128)}, f32[1,2,110,256]{3,2,1,0:T(8,128)}, u32[]{:S(2)}, u32[]{:S(2)}) collective-permute-start(f32[1,2,110,256]{3,2,1,0:T(8,128)} %get-tuple-element.367), channel_id=1, source_target_pairs={{0,1},{1,2},{2,3},{3,4},{4,5},{5,6},{6,7},{7,8},{8,9},{9,10},{10,1... | collective-permute-start | bytes 675848 | tf_op jit(solution)/shard_map/while/body/eval_jaxpr/ppermute | solution.py:67
  236.8 4.4 copy-start.1
  241.1 1.5 copy-start.2
  289.0 21.5 %collective-permute-start = (f32[1,2,110,256]{3,2,1,0:T(8,128)}, f32[1,2,110,256]{3,2,1,0:T(8,128)}, u32[]{:S(2)}, u32[]{:S(2)}) collective-permute-start(f32[1,2,110,256]{3,2,1,0:T(8,128)} %get-tuple-element.367), channel_id=1, source_target_pairs={{1,0},{2,1},{3,2},{4,3},{5,4},{6,5},{7,6},{8,7},{9,8},{10,9},{11,1... | collective-permute-start | bytes 675848 | tf_op jit(solution)/shard_map/while/body/eval_jaxpr/ppermute | solution.py:68
  294.8 15.8 %collective-permute-start.1 = (f32[1,2,110,256]{3,2,1,0:T(8,128)}, f32[1,2,110,256]{3,2,1,0:T(8,128)}, u32[]{:S(2)}, u32[]{:S(2)}) collective-permute-start(f32[1,2,110,256]{3,2,1,0:T(8,128)} %get-tuple-element.367), channel_id=1, source_target_pairs={{0,1},{1,2},{2,3},{3,4},{4,5},{5,6},{6,7},{7,8},{8,9},{9,10},{10,1... | collective-permute-start | bytes 675848 | tf_op jit(solution)/shard_map/while/body/eval_jaxpr/ppermute | solution.py:67
  304.3 4.4 copy-start.1
  308.7 1.5 copy-start.2
  356.6 21.5 %collective-permute-start = (f32[1,2,110,256]{3,2,1,0:T(8,128)}, f32[1,2,110,256]{3,2,1,0:T(8,128)}, u32[]{:S(2)}, u32[]{:S(2)}) collective-permute-start(f32[1,2,110,256]{3,2,1,0:T(8,128)} %get-tuple-element.367), channel_id=1, source_target_pairs={{1,0},{2,1},{3,2},{4,3},{5,4},{6,5},{7,6},{8,7},{9,8},{10,9},{11,1... | collective-permute-start | bytes 675848 | tf_op jit(solution)/shard_map/while/body/eval_jaxpr/ppermute | solution.py:68
  362.3 15.8 %collective-permute-start.1 = (f32[1,2,110,256]{3,2,1,0:T(8,128)}, f32[1,2,110,256]{3,2,1,0:T(8,128)}, u32[]{:S(2)}, u32[]{:S(2)}) collective-permute-start(f32[1,2,110,256]{3,2,1,0:T(8,128)} %get-tuple-element.367), channel_id=1, source_target_pairs={{0,1},{1,2},{2,3},{3,4},{4,5},{5,6},{6,7},{7,8},{8,9},{9,10},{10,1... | collective-permute-start | bytes 675848 | tf_op jit(solution)/shard_map/while/body/eval_jaxpr/ppermute | solution.py:67
  371.9 4.4 copy-start.1
  376.2 1.5 copy-start.2
  424.1 21.5 %collective-permute-start = (f32[1,2,110,256]{3,2,1,0:T(8,128)}, f32[1,2,110,256]{3,2,1,0:T(8,128)}, u32[]{:S(2)}, u32[]{:S(2)}) collective-permute-start(f32[1,2,110,256]{3,2,1,0:T(8,128)} %get-tuple-element.367), channel_id=1, source_target_pairs={{1,0},{2,1},{3,2},{4,3},{5,4},{6,5},{7,6},{8,7},{9,8},{10,9},{11,1... | collective-permute-start | bytes 675848 | tf_op jit(solution)/shard_map/while/body/eval_jaxpr/ppermute | solution.py:68
  429.9 15.8 %collective-permute-start.1 = (f32[1,2,110,256]{3,2,1,0:T(8,128)}, f32[1,2,110,256]{3,2,1,0:T(8,128)}, u32[]{:S(2)}, u32[]{:S(2)}) collective-permute-start(f32[1,2,110,256]{3,2,1,0:T(8,128)} %get-tuple-element.367), channel_id=1, source_target_pairs={{0,1},{1,2},{2,3},{3,4},{4,5},{5,6},{6,7},{7,8},{8,9},{9,10},{10,1... | collective-permute-start | bytes 675848 | tf_op jit(solution)/shard_map/while/body/eval_jaxpr/ppermute | solution.py:67
  439.4 4.4 copy-start.1
  443.8 1.5 copy-start.2
  491.7 21.5 %collective-permute-start = (f32[1,2,110,256]{3,2,1,0:T(8,128)}, f32[1,2,110,256]{3,2,1,0:T(8,128)}, u32[]{:S(2)}, u32[]{:S(2)}) collective-permute-start(f32[1,2,110,256]{3,2,1,0:T(8,128)} %get-tuple-element.367), channel_id=1, source_target_pairs={{1,0},{2,1},{3,2},{4,3},{5,4},{6,5},{7,6},{8,7},{9,8},{10,9},{11,1... | collective-permute-start | bytes 675848 | tf_op jit(solution)/shard_map/while/body/eval_jaxpr/ppermute | solution.py:68
  497.4 15.8 %collective-permute-start.1 = (f32[1,2,110,256]{3,2,1,0:T(8,128)}, f32[1,2,110,256]{3,2,1,0:T(8,128)}, u32[]{:S(2)}, u32[]{:S(2)}) collective-permute-start(f32[1,2,110,256]{3,2,1,0:T(8,128)} %get-tuple-element.367), channel_id=1, source_target_pairs={{0,1},{1,2},{2,3},{3,4},{4,5},{5,6},{6,7},{7,8},{8,9},{9,10},{10,1... | collective-permute-start | bytes 675848 | tf_op jit(solution)/shard_map/while/body/eval_jaxpr/ppermute | solution.py:67
  506.9 4.4 copy-start.1
  559.2 21.5 %collective-permute-start = (f32[1,2,110,256]{3,2,1,0:T(8,128)}, f32[1,2,110,256]{3,2,1,0:T(8,128)}, u32[]{:S(2)}, u32[]{:S(2)}) collective-permute-start(f32[1,2,110,256]{3,2,1,0:T(8,128)} %get-tuple-element.367), channel_id=1, source_target_pairs={{1,0},{2,1},{3,2},{4,3},{5,4},{6,5},{7,6},{8,7},{9,8},{10,9},{11,1... | collective-permute-start | bytes 675848 | tf_op jit(solution)/shard_map/while/body/eval_jaxpr/ppermute | solution.py:68
  565.0 15.8 %collective-permute-start.1 = (f32[1,2,110,256]{3,2,1,0:T(8,128)}, f32[1,2,110,256]{3,2,1,0:T(8,128)}, u32[]{:S(2)}, u32[]{:S(2)}) collective-permute-start(f32[1,2,110,256]{3,2,1,0:T(8,128)} %get-tuple-element.367), channel_id=1, source_target_pairs={{0,1},{1,2},{2,3},{3,4},{4,5},{5,6},{6,7},{7,8},{8,9},{9,10},{10,1... | collective-permute-start | bytes 675848 | tf_op jit(solution)/shard_map/while/body/eval_jaxpr/ppermute | solution.py:67
  574.5 4.4 copy-start.1
  626.7 4.0 copy-start.5
  (19 other events, 28.7 us)
Sparse Core Ops, SparseCore 0:
  9.9 74.1 all-gather.1
